TPU v7x, 512 devices: a whole 4x8x8 slice. The times are simulated.
512 devices in a mesh: wide: 64 (over z, x, core), narrow: 8 (over y).
Axes of the slice: x: 4, y: 8, z: 8, core: 2. Of those that a mesh axis runs over, the one named last changes fastest.
Arguments:
- hidden_in: bfloat16 [16384, 2048], P('wide', 'narrow'), may hold values from -6 to 6
- segment_ids: int32 [16384], P('wide'), may hold values from 0 to 31, never falling along the last dimension, each value on 1 to 2048 neighbouring positions
- page_table: int32 [1024], P('wide'), may hold values from 0 to 1023, as said below
- wq: bfloat16 [2048, 2048], P('wide', 'narrow')
- wk: bfloat16 [2048, 2048], P('wide', 'narrow')
- wv: bfloat16 [2048, 2048], P('wide', 'narrow'), may hold values from -0.125 to 0.125
- wo: bfloat16 [2048, 2048], P('narrow', 'wide'), may hold values from -0.125 to 0.125
- wg: bfloat16 [2048, 4096], P('wide', 'narrow'), may hold values from -0.125 to 0.125
- wu: bfloat16 [2048, 4096], P('wide', 'narrow'), may hold values from -0.125 to 0.125
- wd: bfloat16 [4096, 2048], P('narrow', 'wide'), may hold values from -0.09375 to 0.09375
Outputs:
- result: bfloat16 [16384, 2048], P('wide', 'narrow')
- kv_cache: bfloat16 [2, 1024, 16, 2048], P(None, 'wide', None, 'narrow')
Inputs may be any that keep to these rules, and one draw needn't show every extreme that they name: `page_table`: entries 16 * w to 16 * (w + 1) - 1 of the table are a permutation of those same numbers, for every w.
All inputs are finite; a program needn't handle non-finite values.
Results may differ from a plain program's by a relative error of at most 0.017.
Values may be sent and summed in bfloat16 or wider, within the bound.
No kernel may reach another device: no remote copies, remote signals or barrier semaphores. Data moves between devices by JAX's collectives and lax.ppermute only.
A program may use at most 64 MiB of HBM per device.

v0:
```python
import jax
import jax.numpy as jnp
from jax import lax
from jax.sharding import PartitionSpec as P

HEAD_DIM = 128
REACH = 8
PAGE = 16
epsilon = 1e-05
rope_base = 10000.0


def shifted(value, axis, steps):
    count = lax.axis_size(axis)
    first, last = (max(0, -steps), min(count, count - steps))
    return lax.ppermute(value, axis, [(source, source + steps) for source in range(first, last)])


def norm_rows(source):
    widened = source.astype(jnp.float32)
    center = widened - jnp.mean(widened, axis=-1, keepdims=True)
    spread = jnp.mean(center * center, axis=-1, keepdims=True)
    return (center * lax.rsqrt(spread + epsilon)).astype(jnp.bfloat16)


def rotate(projected, positions):
    head_size = projected.shape[-1]
    half_dim = head_size // 2
    frequency = jnp.power(rope_base, -jnp.arange(half_dim, dtype=jnp.float32) * 2.0 / head_size)
    angles = positions.astype(jnp.float32)[:, None] * frequency[None, :]
    cosine = jnp.cos(angles)[:, None, :]
    sine_part = jnp.sin(angles)[:, None, :]
    first_half = projected[..., :half_dim]
    second_half = projected[..., half_dim:]
    return jnp.concatenate(
        [
            first_half * cosine - second_half * sine_part,
            second_half * cosine + first_half * sine_part,
        ],
        axis=-1,
    )


def add_rows(source, piece):
    return jnp.dot(source, piece, preferred_element_type=jnp.float32)


def per_device(hidden_in, segment_ids, page_table, wq, wk, wv, wo, wg, wu, wd):
    tok_rows = hidden_in.shape[0]
    wide_rank = lax.axis_index("wide")
    local_index = jnp.arange(tok_rows, dtype=jnp.int32)
    attn_width = wq.shape[1]
    ff_width = wg.shape[1]
    pieces = [wq, wk, wv, wo.T, wg, wu, wd.T]
    widths = [piece.shape[1] for piece in pieces]
    gathered = lax.all_gather(jnp.concatenate(pieces, axis=1), "wide", axis=0, tiled=True)
    offsets = [sum(widths[:k]) for k in range(len(widths))]
    full = [gathered[:, o : o + w] for o, w in zip(offsets, widths)]
    wq_all, wk_all, wv_all, wo_t, wg_all, wu_all, wd_t = full
    id_blocks = []
    for step_back in range(REACH, 0, -1):
        got = shifted(segment_ids, "wide", step_back)
        id_blocks.append(jnp.where(wide_rank >= step_back, got, -1))
    id_blocks.append(segment_ids)
    window_ids = jnp.concatenate(id_blocks, axis=0)
    window_len = window_ids.shape[0]
    lead = REACH * tok_rows
    window_index = jnp.arange(window_len, dtype=jnp.int32)
    same = window_ids[None, :] == segment_ids[:, None]
    allowed = same & (window_index[None, :] <= lead + local_index[:, None])
    earlier = same & (window_index[None, :] < lead + local_index[:, None])
    positions = jnp.sum(earlier.astype(jnp.int32), axis=1)
    whole = lax.all_gather(hidden_in, "narrow", axis=1, tiled=True)
    normed = norm_rows(whole)
    local_width = attn_width
    head_count = local_width // HEAD_DIM
    q_proj = add_rows(normed, wq_all)
    k_proj = add_rows(normed, wk_all)
    v_proj = add_rows(normed, wv_all)
    queries = rotate(q_proj.reshape(tok_rows, head_count, HEAD_DIM), positions).astype(jnp.bfloat16)
    keys_rot = rotate(k_proj.reshape(tok_rows, head_count, HEAD_DIM), positions).astype(
        jnp.bfloat16
    )
    values = v_proj.astype(jnp.bfloat16).reshape(tok_rows, head_count, HEAD_DIM)
    blocks = []
    for step_back in range(REACH, 0, -1):
        blocks.append(shifted((keys_rot, values), "wide", step_back))
    blocks.append((keys_rot, values))
    score_scale = HEAD_DIM ** (-0.5)
    key_all = jnp.concatenate([member[0] for member in blocks], axis=0)
    value_all = jnp.concatenate([member[1] for member in blocks], axis=0)
    scores = (
        jnp.einsum("qhd,khd->hqk", queries, key_all, preferred_element_type=jnp.float32)
        * score_scale
    )
    scores = jnp.where(allowed[None], scores, -1e30)
    row_peak = jnp.max(scores, axis=-1, keepdims=True)
    exps = jnp.where(allowed[None], jnp.exp(scores - row_peak), 0.0)
    attn_probs = (exps / jnp.sum(exps, axis=-1, keepdims=True)).astype(jnp.bfloat16)
    mixed = jnp.einsum("hqk,khd->qhd", attn_probs, value_all, preferred_element_type=jnp.float32)
    attended = mixed.astype(jnp.bfloat16).reshape(tok_rows, local_width)
    attn_terms = lax.dot_general(
        attended, wo_t, (((1,), (1,)), ((), ())), preferred_element_type=jnp.float32
    )
    attn_sum = lax.psum_scatter(
        attn_terms.astype(jnp.bfloat16), "narrow", scatter_dimension=1, tiled=True
    ).astype(jnp.float32)
    first_res = (hidden_in.astype(jnp.float32) + attn_sum).astype(jnp.bfloat16)
    whole_two = lax.all_gather(first_res, "narrow", axis=1, tiled=True)
    normed_two = norm_rows(whole_two)
    gate_proj = add_rows(normed_two, wg_all)
    up_proj = add_rows(normed_two, wu_all)
    hidden = (jax.nn.silu(gate_proj) * up_proj).astype(jnp.bfloat16)
    down_terms = lax.dot_general(
        hidden, wd_t, (((1,), (1,)), ((), ())), preferred_element_type=jnp.float32
    )
    down_sum = lax.psum_scatter(
        down_terms.astype(jnp.bfloat16), "narrow", scatter_dimension=1, tiled=True
    ).astype(jnp.float32)
    result = (first_res.astype(jnp.float32) + down_sum).astype(jnp.bfloat16)
    page_count = tok_rows // PAGE
    slots = page_table - wide_rank * page_count
    pairs = jnp.stack(
        [
            keys_rot.reshape(page_count, PAGE, local_width),
            values.reshape(page_count, PAGE, local_width),
        ],
        axis=0,
    )
    kv_cache = jnp.zeros_like(pairs).at[:, slots].set(pairs)
    return (result, kv_cache)


def solution(mesh):
    return jax.shard_map(
        per_device,
        mesh=mesh,
        in_specs=(
            P("wide", "narrow"),
            P("wide"),
            P("wide"),
            P("wide", "narrow"),
            P("wide", "narrow"),
            P("wide", "narrow"),
            P("narrow", "wide"),
            P("wide", "narrow"),
            P("wide", "narrow"),
            P("narrow", "wide"),
        ),
        out_specs=(P("wide", "narrow"), P(None, "wide", None, "narrow")),
        check_vma=False,
    )
```

profile of v0, /device:TPU:6, one launch (start us, length us, event | category | flops | bytes accessed | tf_op | source)
XLA Modules:
  0.0 365.4 jit_solution(13922790470429218336)
XLA Ops:
  13.8 4.3 %collective-permute-start.8 = (s32[256]{0:T(256)}, s32[256]{0:T(256)S(1)}, u32[]{:S(2)}, u32[]{:S(2)}) collective-permute-start(s32[256]{0:T(256)} %param.11), channel_id=1, source_target_pairs={{0,64},{8,72},{16,80},{24,88},{32,96},{40,104},{48,112},{56,120},{... | collective-permute-start | bytes 3080 | tf_op jit(solution)/shard_map/ppermute | solution.py:16
  18.1 3.7 %collective-permute-start.9 = (s32[256]{0:T(256)}, s32[256]{0:T(256)S(1)}, u32[]{:S(2)}, u32[]{:S(2)}) collective-permute-start(s32[256]{0:T(256)} %param.11), channel_id=1, source_target_pairs={{0,56},{8,64},{16,72},{24,80},{32,88},{40,96},{48,104},{56,112},{6... | collective-permute-start | bytes 3080 | tf_op jit(solution)/shard_map/ppermute | solution.py:16
  21.8 4.3 %collective-permute-start.10 = (s32[256]{0:T(256)}, s32[256]{0:T(256)S(1)}, u32[]{:S(2)}, u32[]{:S(2)}) collective-permute-start(s32[256]{0:T(256)} %param.11), channel_id=1, source_target_pairs={{0,48},{8,56},{16,64},{24,72},{32,80},{40,88},{48,96},{56,104},{64... | collective-permute-start | bytes 3080 | tf_op jit(solution)/shard_map/ppermute | solution.py:16
  26.1 6.4 %collective-permute-start.11 = (s32[256]{0:T(256)}, s32[256]{0:T(256)S(1)}, u32[]{:S(2)}, u32[]{:S(2)}) collective-permute-start(s32[256]{0:T(256)} %param.11), channel_id=1, source_target_pairs={{0,40},{8,48},{16,56},{24,64},{32,72},{40,80},{48,88},{56,96},{64,... | collective-permute-start | bytes 3080 | tf_op jit(solution)/shard_map/ppermute | solution.py:16
  32.5 4.3 %collective-permute-start.12 = (s32[256]{0:T(256)}, s32[256]{0:T(256)S(1)}, u32[]{:S(2)}, u32[]{:S(2)}) collective-permute-start(s32[256]{0:T(256)} %param.11), channel_id=1, source_target_pairs={{0,32},{8,40},{16,48},{24,56},{32,64},{40,72},{48,80},{56,88},{64,... | collective-permute-start | bytes 3080 | tf_op jit(solution)/shard_map/ppermute | solution.py:16
  36.9 3.5 collective-permute-start.13
  40.4 2.8 collective-permute-start.14
  43.2 3.4 collective-permute-start.15
  46.8 1.5 collective-permute-done.15
  49.0 1.3 convert_reduce_fusion.2
  50.8 1.4 compare_and_fusion.1
  52.2 4.4 %all-gather.4.cloned.1.call-done = bf16[256,2048]{1,0:T(8,128)(2,1)} async-done(((bf16[256,256]{1,0:T(8,128)(2,1)}), bf16[256,2048]{1,0:T(8,128)(2,1)}) %all-gather.4.cloned.1.call-update) | async-done | bytes 1048592 | tf_op jit(solution)/shard_map/all_gather | solution.py:73
  56.7 1.5 convert_reduce_fusion.1
  58.2 1.6 fusion.12
  59.9 90.5 %all-gather.6.cloned.1.call-done = bf16[2048,2560]{1,0:T(8,128)(2,1)} async-done(((bf16[32,2560]{1,0:T(8,128)(2,1)}), bf16[2048,2560]{1,0:T(8,128)(2,1)}) %all-gather.6.cloned.1.call-update) | async-done | bytes 10485776 | tf_op jit(solution)/shard_map/all_gather | solution.py:56
  150.4 1.9 fusion.29
  152.8 3.4 collective-permute-start.16
  156.2 2.5 collective-permute-start.17
  158.7 4.2 %collective-permute-start.18 = (bf16[256,2,128]{2,0,1:T(8,128)(2,1)S(1)}, bf16[256,2,128]{2,0,1:T(8,128)(2,1)S(1)}, u32[]{:S(2)}, u32[]{:S(2)}) collective-permute-start(bf16[256,2,128]{2,0,1:T(8,128)(2,1)S(1)} %maximum_convert_fusion), channel_id=1, source_target_pairs={{0,48},{8,56},{16,64},{24,72},{32,80},{40,88},{48,96},{56,104},{64... | collective-permute-start | bytes 393224 | tf_op jit(solution)/shard_map/ppermute | solution.py:16
  163.0 4.1 %collective-permute-start.19 = (bf16[256,2,128]{2,0,1:T(8,128)(2,1)S(1)}, bf16[256,2,128]{2,0,1:T(8,128)(2,1)S(1)}, u32[]{:S(2)}, u32[]{:S(2)}) collective-permute-start(bf16[256,2,128]{2,0,1:T(8,128)(2,1)S(1)} %maximum_convert_fusion), channel_id=1, source_target_pairs={{0,40},{8,48},{16,56},{24,64},{32,72},{40,80},{48,88},{56,96},{64,... | collective-permute-start | bytes 393224 | tf_op jit(solution)/shard_map/ppermute | solution.py:16
  167.0 2.8 collective-permute-start.20
  169.8 1.9 fusion.31
  172.0 1.7 convolution_convert_fusion.2
  173.9 3.6 collective-permute-start.21
  177.5 3.5 collective-permute-start.22
  181.1 3.0 collective-permute-start.23
  184.2 2.4 collective-permute-start
  186.6 3.4 collective-permute-start.1
  190.1 3.2 collective-permute-start.2
  193.3 2.2 collective-permute-start.3
  195.6 3.6 collective-permute-start.4
  200.2 3.5 collective-permute-start.5
  203.8 2.3 collective-permute-start.6
  206.1 3.5 collective-permute-start.7
  209.8 1.8 collective-permute-done.6
  213.8 4.7 %fusion.62 = (f32[2,256]{1,0:T(2,128)S(1)}, f32[2,256,2304]{2,1,0:T(8,128)}) fusion(bf16[2304,2,128]{2,0,1:T(8,128)(2,1)S(1)} %copy-done.7, pred[256,2304]{1,0:T(8,128)(4,1)S(1)} %compare_and_fusion.1, bf16[256,2,64]{2,0,1:T(8,128)(2,1)S(1)} %get-tuple-element.3, bf16[256,2,64]{2,0,1:T(8,128)(2,1)S(1)} %get-tuple-element.2), kind=kOutput, calls=%fused_computation.111 | convolution fusion | flops 308152576 | bytes 6621184 | tf_op jit(solution)/shard_map/sub | solution.py:98
  218.5 3.7 %fusion.27 = bf16[2,128,256]{2,1,0:T(8,128)(2,1)S(1)} fusion(bf16[2304,2,128]{0,2,1:T(8,128)(2,1)} %copy-done.8, f32[2,256,2304]{2,1,0:T(8,128)} %get-tuple-element.13, f32[2,256]{1,0:T(2,128)S(1)} %get-tuple-element.12), kind=kOutput, calls=%fused_computation.35 | convolution fusion | flops 304414720 | bytes 6031360 | tf_op jit(solution)/shard_map/hqk,khd->qhd/dot_general | solution.py:100
  222.2 2.8 convolution_convert_fusion.1
  225.0 37.6 %reduce-scatter.3.cloned.1.call-done = bf16[256,256]{1,0:T(8,128)(2,1)} async-done(((bf16[256,2048]{1,0:T(8,128)(2,1)}), bf16[256,256]{1,0:T(8,128)(2,1)}) %reduce-scatter.3.cloned.1.call-update) | async-done | bytes 131088 | tf_op jit(solution)/shard_map/reduce_scatter | solution.py:105
  262.6 1.6 add_convert_fusion.1
  264.4 42.0 %all-gather.8.cloned.1.call-done = bf16[256,2048]{1,0:T(8,128)(2,1)} async-done(((bf16[256,256]{1,0:T(8,128)(2,1)}), bf16[256,2048]{1,0:T(8,128)(2,1)}) %all-gather.8.cloned.1.call-update) | async-done | bytes 1048592 | tf_op jit(solution)/shard_map/all_gather | solution.py:109
  306.4 1.5 convert_reduce_fusion
  307.9 1.6 fusion.10
  309.6 2.3 fusion.17
  312.0 4.7 %convolution_convert_fusion = bf16[256,2048]{1,0:T(8,128)(2,1)} fusion(bf16[2048,2560]{1,0:T(8,128)(2,1)} %all-gather.6.cloned.1.call-done, f32[256,512]{1,0:T(8,128)S(1)} %fusion.17, bf16[256,2048]{1,0:T(8,128)(2,1)S(1)} %copy-done.1, f32[256]{0:T(256)S(1)} %add_rsqrt_fusion, f32[256]{0:T(256)S(1)} %broadcast_multiply_fusion), kind=kOutput, calls=%fused_computation.14 | convolution fusion | flops 1077149696 | bytes 6817792 | tf_op jit(solution)/shard_map/dot_general | solution.py:114
  317.0 1.2 scatter_fusion
  318.2 39.1 %reduce-scatter.5.cloned.1.call-done = bf16[256,256]{1,0:T(8,128)(2,1)} async-done(((bf16[256,2048]{1,0:T(8,128)(2,1)}), bf16[256,256]{1,0:T(8,128)(2,1)}) %reduce-scatter.5.cloned.1.call-update) | async-done | bytes 131088 | tf_op jit(solution)/shard_map/reduce_scatter | solution.py:117
  357.3 1.6 add_convert_fusion
  (111 shorter events, 13.0 us)
Async XLA Ops:
  7.2 49.5 %all-gather.4.cloned.1.call-start = ((), (), s32[]{:S(2)}) async-start(), calls=%async_computation.2 | async-start | bytes 1179648 | tf_op jit(solution)/shard_map/all_gather | solution.py:73
  7.9 142.5 %all-gather.6.cloned.1.call-start = ((), (), s32[]{:S(2)}) async-start(), calls=%async_computation.3 | async-start | bytes 10649600 | tf_op jit(solution)/shard_map/all_gather | solution.py:56
  13.1 0.7 copy-start.5
  13.8 248.8 %reduce-scatter.3.cloned.1.call-start = ((), (), s32[]{:S(2)}) async-start(), calls=%async_computation.4 | async-start | bytes 1179648 | tf_op jit(solution)/shard_map/reduce_scatter | solution.py:105
  13.8 23.0 %collective-permute-start.8 = (s32[256]{0:T(256)}, s32[256]{0:T(256)S(1)}, u32[]{:S(2)}, u32[]{:S(2)}) collective-permute-start(s32[256]{0:T(256)} %param.11), channel_id=1, source_target_pairs={{0,64},{8,72},{16,80},{24,88},{32,96},{40,104},{48,112},{56,120},{... | collective-permute-start | bytes 3080 | tf_op jit(solution)/shard_map/ppermute | solution.py:16
  18.1 22.2 %collective-permute-start.9 = (s32[256]{0:T(256)}, s32[256]{0:T(256)S(1)}, u32[]{:S(2)}, u32[]{:S(2)}) collective-permute-start(s32[256]{0:T(256)} %param.11), channel_id=1, source_target_pairs={{0,56},{8,64},{16,72},{24,80},{32,88},{40,96},{48,104},{56,112},{6... | collective-permute-start | bytes 3080 | tf_op jit(solution)/shard_map/ppermute | solution.py:16
  21.8 21.3 %collective-permute-start.10 = (s32[256]{0:T(256)}, s32[256]{0:T(256)S(1)}, u32[]{:S(2)}, u32[]{:S(2)}) collective-permute-start(s32[256]{0:T(256)} %param.11), channel_id=1, source_target_pairs={{0,48},{8,56},{16,64},{24,72},{32,80},{40,88},{48,96},{56,104},{64... | collective-permute-start | bytes 3080 | tf_op jit(solution)/shard_map/ppermute | solution.py:16
  26.1 20.5 %collective-permute-start.11 = (s32[256]{0:T(256)}, s32[256]{0:T(256)S(1)}, u32[]{:S(2)}, u32[]{:S(2)}) collective-permute-start(s32[256]{0:T(256)} %param.11), channel_id=1, source_target_pairs={{0,40},{8,48},{16,56},{24,64},{32,72},{40,80},{48,88},{56,96},{64,... | collective-permute-start | bytes 3080 | tf_op jit(solution)/shard_map/ppermute | solution.py:16
  32.5 14.2 %collective-permute-start.12 = (s32[256]{0:T(256)}, s32[256]{0:T(256)S(1)}, u32[]{:S(2)}, u32[]{:S(2)}) collective-permute-start(s32[256]{0:T(256)} %param.11), channel_id=1, source_target_pairs={{0,32},{8,40},{16,48},{24,56},{32,64},{40,72},{48,80},{56,88},{64,... | collective-permute-start | bytes 3080 | tf_op jit(solution)/shard_map/ppermute | solution.py:16
  36.9 9.8 %collective-permute-start.13 = (s32[256]{0:T(256)}, s32[256]{0:T(256)S(1)}, u32[]{:S(2)}, u32[]{:S(2)}) collective-permute-start(s32[256]{0:T(256)} %param.11), channel_id=1, source_target_pairs={{0,24},{8,32},{16,40},{24,48},{32,56},{40,64},{48,72},{56,80},{64,... | collective-permute-start | bytes 3080 | tf_op jit(solution)/shard_map/ppermute | solution.py:16
  40.4 6.3 %collective-permute-start.14 = (s32[256]{0:T(256)}, s32[256]{0:T(256)S(1)}, u32[]{:S(2)}, u32[]{:S(2)}) collective-permute-start(s32[256]{0:T(256)} %param.11), channel_id=1, source_target_pairs={{0,16},{8,24},{16,32},{24,40},{32,48},{40,56},{48,64},{56,72},{64,... | collective-permute-start | bytes 3080 | tf_op jit(solution)/shard_map/ppermute | solution.py:16
  43.2 5.1 %collective-permute-start.15 = (s32[256]{0:T(256)}, s32[256]{0:T(256)S(1)}, u32[]{:S(2)}, u32[]{:S(2)}) collective-permute-start(s32[256]{0:T(256)} %param.11), channel_id=1, source_target_pairs={{0,8},{8,16},{16,24},{24,32},{32,40},{40,48},{48,56},{56,64},{64,7... | collective-permute-start | bytes 3080 | tf_op jit(solution)/shard_map/ppermute | solution.py:16
  56.7 93.7 %copy-start = (bf16[256,2048]{1,0:T(8,128)(2,1)S(1)}, bf16[256,2048]{1,0:T(8,128)(2,1)}, u32[]{:S(2)}) copy-start(bf16[256,2048]{1,0:T(8,128)(2,1)} %all-gather.4.cloned.1.call-done) | copy-start | bytes 3145732
  152.8 21.1 %collective-permute-start.16 = (bf16[256,2,128]{2,0,1:T(8,128)(2,1)S(1)}, bf16[256,2,128]{2,0,1:T(8,128)(2,1)S(1)}, u32[]{:S(2)}, u32[]{:S(2)}) collective-permute-start(bf16[256,2,128]{2,0,1:T(8,128)(2,1)S(1)} %maximum_convert_fusion), channel_id=1, source_target_pairs={{0,64},{8,72},{16,80},{24,88},{32,96},{40,104},{48,112},{56,120},{... | collective-permute-start | bytes 393224 | tf_op jit(solution)/shard_map/ppermute | solution.py:16
  156.2 21.3 %collective-permute-start.17 = (bf16[256,2,128]{2,0,1:T(8,128)(2,1)S(1)}, bf16[256,2,128]{2,0,1:T(8,128)(2,1)S(1)}, u32[]{:S(2)}, u32[]{:S(2)}) collective-permute-start(bf16[256,2,128]{2,0,1:T(8,128)(2,1)S(1)} %maximum_convert_fusion), channel_id=1, source_target_pairs={{0,56},{8,64},{16,72},{24,80},{32,88},{40,96},{48,104},{56,112},{6... | collective-permute-start | bytes 393224 | tf_op jit(solution)/shard_map/ppermute | solution.py:16
  158.7 22.3 %collective-permute-start.18 = (bf16[256,2,128]{2,0,1:T(8,128)(2,1)S(1)}, bf16[256,2,128]{2,0,1:T(8,128)(2,1)S(1)}, u32[]{:S(2)}, u32[]{:S(2)}) collective-permute-start(bf16[256,2,128]{2,0,1:T(8,128)(2,1)S(1)} %maximum_convert_fusion), channel_id=1, source_target_pairs={{0,48},{8,56},{16,64},{24,72},{32,80},{40,88},{48,96},{56,104},{64... | collective-permute-start | bytes 393224 | tf_op jit(solution)/shard_map/ppermute | solution.py:16
  163.0 21.2 %collective-permute-start.19 = (bf16[256,2,128]{2,0,1:T(8,128)(2,1)S(1)}, bf16[256,2,128]{2,0,1:T(8,128)(2,1)S(1)}, u32[]{:S(2)}, u32[]{:S(2)}) collective-permute-start(bf16[256,2,128]{2,0,1:T(8,128)(2,1)S(1)} %maximum_convert_fusion), channel_id=1, source_target_pairs={{0,40},{8,48},{16,56},{24,64},{32,72},{40,80},{48,88},{56,96},{64,... | collective-permute-start | bytes 393224 | tf_op jit(solution)/shard_map/ppermute | solution.py:16
  167.0 19.5 %collective-permute-start.20 = (bf16[256,2,128]{2,0,1:T(8,128)(2,1)S(1)}, bf16[256,2,128]{2,0,1:T(8,128)(2,1)S(1)}, u32[]{:S(2)}, u32[]{:S(2)}) collective-permute-start(bf16[256,2,128]{2,0,1:T(8,128)(2,1)S(1)} %maximum_convert_fusion), channel_id=1, source_target_pairs={{0,32},{8,40},{16,48},{24,56},{32,64},{40,72},{48,80},{56,88},{64,... | collective-permute-start | bytes 393224 | tf_op jit(solution)/shard_map/ppermute | solution.py:16
  173.9 16.1 %collective-permute-start.21 = (bf16[256,2,128]{2,0,1:T(8,128)(2,1)S(1)}, bf16[256,2,128]{2,0,1:T(8,128)(2,1)S(1)}, u32[]{:S(2)}, u32[]{:S(2)}) collective-permute-start(bf16[256,2,128]{2,0,1:T(8,128)(2,1)S(1)} %maximum_convert_fusion), channel_id=1, source_target_pairs={{0,24},{8,32},{16,40},{24,48},{32,56},{40,64},{48,72},{56,80},{64,... | collective-permute-start | bytes 393224 | tf_op jit(solution)/shard_map/ppermute | solution.py:16
  177.5 15.7 %collective-permute-start.22 = (bf16[256,2,128]{2,0,1:T(8,128)(2,1)S(1)}, bf16[256,2,128]{2,0,1:T(8,128)(2,1)S(1)}, u32[]{:S(2)}, u32[]{:S(2)}) collective-permute-start(bf16[256,2,128]{2,0,1:T(8,128)(2,1)S(1)} %maximum_convert_fusion), channel_id=1, source_target_pairs={{0,16},{8,24},{16,32},{24,40},{32,48},{40,56},{48,64},{56,72},{64,... | collective-permute-start | bytes 393224 | tf_op jit(solution)/shard_map/ppermute | solution.py:16
  181.1 14.5 %collective-permute-start.23 = (bf16[256,2,128]{2,0,1:T(8,128)(2,1)S(1)}, bf16[256,2,128]{2,0,1:T(8,128)(2,1)S(1)}, u32[]{:S(2)}, u32[]{:S(2)}) collective-permute-start(bf16[256,2,128]{2,0,1:T(8,128)(2,1)S(1)} %maximum_convert_fusion), channel_id=1, source_target_pairs={{0,8},{8,16},{16,24},{24,32},{32,40},{40,48},{48,56},{56,64},{64,7... | collective-permute-start | bytes 393224 | tf_op jit(solution)/shard_map/ppermute | solution.py:16
  184.2 16.1 %collective-permute-start = (bf16[256,2,128]{0,2,1:T(8,128)(2,1)S(1)}, bf16[256,2,128]{0,2,1:T(8,128)(2,1)S(1)}, u32[]{:S(2)}, u32[]{:S(2)}) collective-permute-start(bf16[256,2,128]{0,2,1:T(8,128)(2,1)S(1)} %bitcast.16), channel_id=1, source_target_pairs={{0,64},{8,72},{16,80},{24,88},{32,96},{40,104},{48,112},{56,120},{... | collective-permute-start | bytes 393224 | tf_op jit(solution)/shard_map/ppermute | solution.py:16
  186.6 17.2 %collective-permute-start.1 = (bf16[256,2,128]{0,2,1:T(8,128)(2,1)S(1)}, bf16[256,2,128]{0,2,1:T(8,128)(2,1)S(1)}, u32[]{:S(2)}, u32[]{:S(2)}) collective-permute-start(bf16[256,2,128]{0,2,1:T(8,128)(2,1)S(1)} %bitcast.17), channel_id=1, source_target_pairs={{0,56},{8,64},{16,72},{24,80},{32,88},{40,96},{48,104},{56,112},{6... | collective-permute-start | bytes 393224 | tf_op jit(solution)/shard_map/ppermute | solution.py:16
  190.1 16.0 %collective-permute-start.2 = (bf16[256,2,128]{0,2,1:T(8,128)(2,1)S(1)}, bf16[256,2,128]{0,2,1:T(8,128)(2,1)S(1)}, u32[]{:S(2)}, u32[]{:S(2)}) collective-permute-start(bf16[256,2,128]{0,2,1:T(8,128)(2,1)S(1)} %bitcast.18), channel_id=1, source_target_pairs={{0,48},{8,56},{16,64},{24,72},{32,80},{40,88},{48,96},{56,104},{64... | collective-permute-start | bytes 393224 | tf_op jit(solution)/shard_map/ppermute | solution.py:16
  193.3 16.4 %collective-permute-start.3 = (bf16[256,2,128]{0,2,1:T(8,128)(2,1)S(1)}, bf16[256,2,128]{0,2,1:T(8,128)(2,1)S(1)}, u32[]{:S(2)}, u32[]{:S(2)}) collective-permute-start(bf16[256,2,128]{0,2,1:T(8,128)(2,1)S(1)} %bitcast.19), channel_id=1, source_target_pairs={{0,40},{8,48},{16,56},{24,64},{32,72},{40,80},{48,88},{56,96},{64,... | collective-permute-start | bytes 393224 | tf_op jit(solution)/shard_map/ppermute | solution.py:16
  195.6 14.2 %collective-permute-start.4 = (bf16[256,2,128]{0,2,1:T(8,128)(2,1)S(1)}, bf16[256,2,128]{0,2,1:T(8,128)(2,1)S(1)}, u32[]{:S(2)}, u32[]{:S(2)}) collective-permute-start(bf16[256,2,128]{0,2,1:T(8,128)(2,1)S(1)} %bitcast.20), channel_id=1, source_target_pairs={{0,32},{8,40},{16,48},{24,56},{32,64},{40,72},{48,80},{56,88},{64,... | collective-permute-start | bytes 393224 | tf_op jit(solution)/shard_map/ppermute | solution.py:16
  199.2 1.0 copy-start.6
  200.2 13.6 %copy-start.7 = (bf16[2304,2,128]{2,0,1:T(8,128)(2,1)S(1)}, bf16[2304,2,128]{2,0,1:T(8,128)(2,1)}, u32[]{:S(2)}) copy-start(bf16[2304,2,128]{2,0,1:T(8,128)(2,1)} %copy-done.6) | copy-start | bytes 3538948
  200.2 9.5 %collective-permute-start.5 = (bf16[256,2,128]{0,2,1:T(8,128)(2,1)S(1)}, bf16[256,2,128]{0,2,1:T(8,128)(2,1)S(1)}, u32[]{:S(2)}, u32[]{:S(2)}) collective-permute-start(bf16[256,2,128]{0,2,1:T(8,128)(2,1)S(1)} %bitcast.21), channel_id=1, source_target_pairs={{0,24},{8,32},{16,40},{24,48},{32,56},{40,64},{48,72},{56,80},{64,... | collective-permute-start | bytes 393224 | tf_op jit(solution)/shard_map/ppermute | solution.py:16
  203.8 7.8 %collective-permute-start.6 = (bf16[256,2,128]{0,2,1:T(8,128)(2,1)S(1)}, bf16[256,2,128]{0,2,1:T(8,128)(2,1)S(1)}, u32[]{:S(2)}, u32[]{:S(2)}) collective-permute-start(bf16[256,2,128]{0,2,1:T(8,128)(2,1)S(1)} %bitcast.22), channel_id=1, source_target_pairs={{0,16},{8,24},{16,32},{24,40},{32,48},{40,56},{48,64},{56,72},{64,... | collective-permute-start | bytes 393224 | tf_op jit(solution)/shard_map/ppermute | solution.py:16
  206.1 6.6 %collective-permute-start.7 = (bf16[256,2,128]{0,2,1:T(8,128)(2,1)S(1)}, bf16[256,2,128]{0,2,1:T(8,128)(2,1)S(1)}, u32[]{:S(2)}, u32[]{:S(2)}) collective-permute-start(bf16[256,2,128]{0,2,1:T(8,128)(2,1)S(1)} %bitcast.23), channel_id=1, source_target_pairs={{0,8},{8,16},{16,24},{24,32},{32,40},{40,48},{48,56},{56,64},{64,7... | collective-permute-start | bytes 393224 | tf_op jit(solution)/shard_map/ppermute | solution.py:16
  212.7 1.0 copy-start.8
  222.2 40.4 %copy-start.4 = (bf16[256,256]{1,0:T(8,128)(2,1)S(1)}, bf16[256,256]{1,0:T(8,128)(2,1)}, u32[]{:S(2)}) copy-start(bf16[256,256]{1,0:T(8,128)(2,1)} %param.10) | copy-start | bytes 393220
  225.0 81.4 %all-gather.8.cloned.1.call-start = ((), (), s32[]{:S(2)}) async-start(), calls=%async_computation.5 | async-start | bytes 1179648 | tf_op jit(solution)/shard_map/all_gather | solution.py:109
  264.2 93.1 %reduce-scatter.5.cloned.1.call-start = ((), (), s32[]{:S(2)}) async-start(), calls=%async_computation.6 | async-start | bytes 1179648 | tf_op jit(solution)/shard_map/reduce_scatter | solution.py:117
  306.4 3.2 copy-start.1
  311.9 4.7 %copy-start.9 = (s32[16]{0:T(128)S(1)}, s32[16]{0:T(128)}, u32[]{:S(2)}) copy-start(s32[16]{0:T(128)} %param.12) | copy-start | bytes 196
  316.6 40.7 %copy-start.2 = (bf16[256,256]{1,0:T(8,128)(2,1)S(1)}, bf16[256,256]{1,0:T(8,128)(2,1)}, u32[]{:S(2)}) copy-start(bf16[256,256]{1,0:T(8,128)(2,1)} %add_convert_fusion.1) | copy-start | bytes 393220
  318.2 40.7 %copy-start.3 = (bf16[2,16,16,256]{3,2,1,0:T(8,128)(2,1)}, bf16[2,16,16,256]{3,2,1,0:T(8,128)(2,1)S(1)}, u32[]{:S(2)}) copy-start(bf16[2,16,16,256]{3,2,1,0:T(8,128)(2,1)S(1)} %scatter_fusion) | copy-start | bytes 786436
Sparse Core Ops, SparseCore 0:
  10.0 46.6 all-gather.3
  60.6 89.7 all-gather.5
  225.1 37.4 reduce-scatter.2
  265.0 41.3 all-gather.7
  316.8 40.5 reduce-scatter.4
where the time goes:
time: 367 us; the launch traced here: 365 us
  waiting for transfers between devices  219 us (60%)
  starting transfers between devices  84.2 us (23%)
  matrix products  23.6 us (6%)
  between operations  14.6 us (4%)
  other arithmetic  13.2 us (4%)
  local copies, waits for them, and re-layouts  11 us (3%)
    all_gather x1, waiting for transfers between devices, per_device(): lax.all_gather(jnp.concatenate(pieces, axis=1), 'wide', axis=0, tiled=True)  90.5 us
    ppermute x24, starting transfers between devices, shifted(): lax.ppermute(value, axis, [(source, source + steps) for source in range(f...  83.8 us
    all_gather x1, waiting for transfers between devices, per_device(): whole_two = lax.all_gather(first_res, 'narrow', axis=1, tiled=True)  42 us
    reduce_scatter x1, waiting for transfers between devices, per_device(): lax.psum_scatter(down_terms.astype(jnp.bfloat16), 'narrow', scatter_dimen...  39.1 us
    reduce_scatter x1, waiting for transfers between devices, per_device(): lax.psum_scatter(attn_terms.astype(jnp.bfloat16), 'narrow', scatter_dimen...  37.6 us
    unnamed x46, local copies, waits for them, and re-layouts  7.88 us
    dot_general x4, matrix products, add_rows(): return jnp.dot(source, piece, preferred_element_type=jnp.float32)  7.84 us
  transfers between devices with their start and end apart: 29, of which 8 were waited for; matrix products, arithmetic and copies ran while one was open for 5% of the time, Pallas kernels for 0%

commit v1 on v0

--- a/solution.py
+++ b/solution.py
@@ -53,7 +53,12 @@
     ff_width = wg.shape[1]
     pieces = [wq, wk, wv, wo.T, wg, wu, wd.T]
     widths = [piece.shape[1] for piece in pieces]
-    gathered = lax.all_gather(jnp.concatenate(pieces, axis=1), "wide", axis=0, tiled=True)
+    gathered = jnp.concatenate(
+        lax.all_to_all(
+            jnp.stack([jnp.concatenate(pieces, axis=1)] * lax.axis_size("wide")), "wide", 0, 0
+        ),
+        axis=0,
+    )
     offsets = [sum(widths[:k]) for k in range(len(widths))]
     full = [gathered[:, o : o + w] for o, w in zip(offsets, widths)]
     wq_all, wk_all, wv_all, wo_t, wg_all, wu_all, wd_t = full

time: 367 us -> 494 us (1.35)
  waiting for transfers between devices: 219 us -> 328 us
  starting transfers between devices: 84.2 us -> 99.2 us
    ppermute x24, waiting for transfers between devices: 4.52 us -> 208 us  [shifted(): lax.ppermute(value, axis, [(source, source + steps) for source in range(f...]
    all_gather x1 -> x0, waiting for transfers between devices: 90.5 us -> none  [per_device(): lax.all_gather(jnp.concatenate(pieces, axis=1), 'wide', axis=0, tiled=True)]
    all_to_all x0 -> x1, starting transfers between devices: none -> 14.1 us  [per_device(): lax.all_to_all(jnp.stack([jnp.concatenate(pieces, axis=1)] * lax.axis_siz...]
    another operation x0 -> x1, local copies, waits for them, and re-layouts: none -> 5.11 us  [per_device(): jnp.stack([jnp.concatenate(pieces, axis=1)] * lax.axis_size('wide'))]
  transfers between devices with their start and end apart: 29 -> 29, of which waited for: 8 -> 7; matrix products, arithmetic and copies ran while one was open for 5% -> 2% of each run, Pallas kernels for 0% -> 0%
where the time goes in v1:
time: 494 us; the launch traced here: 492 us
  waiting for transfers between devices  328 us (66%)
  starting transfers between devices  99.2 us (20%)
  matrix products  24.6 us (5%)
  between operations  14.7 us (3%)
  local copies, waits for them, and re-layouts  13.7 us (3%)
  other arithmetic  11.9 us (2%)
    ppermute x24, waiting for transfers between devices, shifted(): lax.ppermute(value, axis, [(source, source + steps) for source in range(f...  208 us
    ppermute x24, starting transfers between devices, shifted(): lax.ppermute(value, axis, [(source, source + steps) for source in range(f...  84.9 us
    all_gather x1, waiting for transfers between devices, per_device(): whole_two = lax.all_gather(first_res, 'narrow', axis=1, tiled=True)  42.3 us
    reduce_scatter x1, waiting for transfers between devices, per_device(): lax.psum_scatter(down_terms.astype(jnp.bfloat16), 'narrow', scatter_dimen...  39 us
    reduce_scatter x1, waiting for transfers between devices, per_device(): lax.psum_scatter(attn_terms.astype(jnp.bfloat16), 'narrow', scatter_dimen...  38.2 us
    all_to_all x1, starting transfers between devices, per_device(): lax.all_to_all(jnp.stack([jnp.concatenate(pieces, axis=1)] * lax.axis_siz...  14.1 us
  transfers between devices with their start and end apart: 29, of which 7 were waited for; matrix products, arithmetic and copies ran while one was open for 2% of the time, Pallas kernels for 0%

profile of v1, /device:TPU:6, one launch (start us, length us, event | category | flops | bytes accessed | tf_op | source)
XLA Modules:
  0.0 492.0 jit_solution(3044305114060533244)
XLA Ops:
  12.3 5.1 %stack.4 = bf16[64,32,2560]{2,1,0:T(8,128)(2,1)} broadcast(bf16[32,2560]{1,0:T(8,128)(2,1)S(1)} %constant_dynamic-update-slice_fusion), dimensions={1,2} | broadcast | bytes 10649600 | tf_op jit(solution)/shard_map/stack | solution.py:58
  17.4 14.1 %all-to-all-start = ((bf16[64,32,2560]{2,1,0:T(8,128)(2,1)}), bf16[64,32,2560]{2,1,0:T(8,128)(2,1)}, u32[]{:S(2)}, u32[]{:S(2)}) async-start(bf16[64,32,2560]{2,1,0:T(8,128)(2,1)} %stack.4), calls=%async_computation | async-start | bytes 20971520 | tf_op jit(solution)/shard_map/all_to_all | solution.py:57
  31.6 3.4 collective-permute-start.8
  35.0 3.1 collective-permute-start.9
  38.1 3.4 collective-permute-start.10
  41.6 5.2 %collective-permute-start.11 = (s32[256]{0:T(256)S(1)}, s32[256]{0:T(256)S(1)}, u32[]{:S(2)}, u32[]{:S(2)}) collective-permute-start(s32[256]{0:T(256)S(1)} %copy-done.8), channel_id=1, source_target_pairs={{0,40},{8,48},{16,56},{24,64},{32,72},{40,80},{48,88},{56,96},{64,... | collective-permute-start | bytes 3080 | tf_op jit(solution)/shard_map/ppermute | solution.py:16
  46.8 4.3 collective-permute-start.12
  51.2 203.2 %collective-permute-done.8 = s32[256]{0:T(256)S(1)} collective-permute-done((s32[256]{0:T(256)S(1)}, s32[256]{0:T(256)S(1)}, u32[]{:S(2)}, u32[]{:S(2)}) %collective-permute-start.8) | collective-permute-done | bytes 1056 | tf_op jit(solution)/shard_map/ppermute | solution.py:16
  254.4 2.8 collective-permute-start.13
  257.2 6.9 %collective-permute-start.14 = (s32[256]{0:T(256)S(1)}, s32[256]{0:T(256)S(1)}, u32[]{:S(2)}, u32[]{:S(2)}) collective-permute-start(s32[256]{0:T(256)S(1)} %copy-done.8), channel_id=1, source_target_pairs={{0,16},{8,24},{16,32},{24,40},{32,48},{40,56},{48,64},{56,72},{64,... | collective-permute-start | bytes 3080 | tf_op jit(solution)/shard_map/ppermute | solution.py:16
  264.1 3.1 collective-permute-start.15
  267.4 2.5 collective-permute-done.15
  271.8 1.5 convert_reduce_fusion.1
  273.4 1.6 fusion.12
  275.1 1.7 convolution_convert_fusion.2
  276.9 4.5 collective-permute-start
  281.3 1.3 collective-permute-start.1
  282.7 3.2 collective-permute-start.2
  285.9 7.4 %collective-permute-start.3 = (bf16[256,2,128]{0,2,1:T(8,128)(2,1)S(1)}, bf16[256,2,128]{0,2,1:T(8,128)(2,1)S(1)}, u32[]{:S(2)}, u32[]{:S(2)}) collective-permute-start(bf16[256,2,128]{0,2,1:T(8,128)(2,1)S(1)} %bitcast.20), channel_id=1, source_target_pairs={{0,40},{8,48},{16,56},{24,64},{32,72},{40,80},{48,88},{56,96},{64,... | collective-permute-start | bytes 393224 | tf_op jit(solution)/shard_map/ppermute | solution.py:16
  293.3 2.3 collective-permute-start.4
  295.5 1.9 fusion.29
  297.7 1.9 fusion.31
  300.2 3.6 collective-permute-start.5
  303.9 2.8 collective-permute-start.6
  306.7 3.1 collective-permute-start.7
  309.8 2.3 collective-permute-start.16
  312.1 4.3 collective-permute-start.17
  316.5 2.8 collective-permute-start.18
  319.3 1.9 collective-permute-start.19
  321.3 4.3 collective-permute-start.20
  325.7 2.8 collective-permute-start.21
  328.5 2.8 collective-permute-start.22
  331.3 3.4 collective-permute-start.23
  334.9 1.3 collective-permute-done.22
  336.2 1.4 collective-permute-done.23
  338.7 6.0 %fusion.62 = (f32[2,256]{1,0:T(2,128)S(1)}, f32[2,256,2304]{2,1,0:T(8,128)}) fusion(bf16[2304,2,128]{2,0,1:T(8,128)(2,1)} %copy-done.7, pred[256,2304]{1,0:T(8,128)(4,1)S(1)} %compare_and_fusion.1, bf16[256,2,64]{2,0,1:T(8,128)(2,1)S(1)} %get-tuple-element.3, bf16[256,2,64]{2,0,1:T(8,128)(2,1)S(1)} %get-tuple-element.2), kind=kOutput, calls=%fused_computation.111 | convolution fusion | flops 308152576 | bytes 6621184 | tf_op jit(solution)/shard_map/sub | solution.py:103
  344.7 3.3 fusion.27
  348.1 2.8 convolution_convert_fusion.1
  350.9 38.2 %reduce-scatter.3.cloned.1.call-done = bf16[256,256]{1,0:T(8,128)(2,1)} async-done(((bf16[256,2048]{1,0:T(8,128)(2,1)}), bf16[256,256]{1,0:T(8,128)(2,1)}) %reduce-scatter.3.cloned.1.call-update) | async-done | bytes 131088 | tf_op jit(solution)/shard_map/reduce_scatter | solution.py:110
  389.1 1.6 add_convert_fusion.1
  390.8 42.3 %all-gather.5.cloned.1.call-done = bf16[256,2048]{1,0:T(8,128)(2,1)} async-done(((bf16[256,256]{1,0:T(8,128)(2,1)}), bf16[256,2048]{1,0:T(8,128)(2,1)}) %all-gather.5.cloned.1.call-update) | async-done | bytes 1048592 | tf_op jit(solution)/shard_map/all_gather | solution.py:114
  433.1 1.5 convert_reduce_fusion
  434.6 1.6 fusion.10
  436.3 2.3 fusion.17
  438.7 4.7 convolution_convert_fusion
  443.7 1.2 scatter_fusion
  444.9 39.0 %reduce-scatter.5.cloned.1.call-done = bf16[256,256]{1,0:T(8,128)(2,1)} async-done(((bf16[256,2048]{1,0:T(8,128)(2,1)}), bf16[256,256]{1,0:T(8,128)(2,1)}) %reduce-scatter.5.cloned.1.call-update) | async-done | bytes 131088 | tf_op jit(solution)/shard_map/reduce_scatter | solution.py:122
  483.9 1.6 add_convert_fusion
  (111 shorter events, 10.0 us)
Async XLA Ops:
  17.4 14.2 %copy-start.8 = (s32[256]{0:T(256)S(1)}, s32[256]{0:T(256)}, u32[]{:S(2)}) copy-start(s32[256]{0:T(256)} %param.11) | copy-start | bytes 3076
  17.4 257.6 %all-to-all-start = ((bf16[64,32,2560]{2,1,0:T(8,128)(2,1)}), bf16[64,32,2560]{2,1,0:T(8,128)(2,1)}, u32[]{:S(2)}, u32[]{:S(2)}) async-start(bf16[64,32,2560]{2,1,0:T(8,128)(2,1)} %stack.4), calls=%async_computation | async-start | bytes 20971520 | tf_op jit(solution)/shard_map/all_to_all | solution.py:57
  31.6 240.3 %all-gather.3.cloned.1.call-start = ((), (), s32[]{:S(2)}) async-start(), calls=%async_computation.3 | async-start | bytes 1179648 | tf_op jit(solution)/shard_map/all_gather | solution.py:78
  31.6 222.8 %collective-permute-start.8 = (s32[256]{0:T(256)S(1)}, s32[256]{0:T(256)S(1)}, u32[]{:S(2)}, u32[]{:S(2)}) collective-permute-start(s32[256]{0:T(256)S(1)} %copy-done.8), channel_id=1, source_target_pairs={{0,64},{8,72},{16,80},{24,88},{32,96},{40,104},{48,112},{56,120},{... | collective-permute-start | bytes 3080 | tf_op jit(solution)/shard_map/ppermute | solution.py:16
  35.0 222.2 %collective-permute-start.9 = (s32[256]{0:T(256)S(1)}, s32[256]{0:T(256)S(1)}, u32[]{:S(2)}, u32[]{:S(2)}) collective-permute-start(s32[256]{0:T(256)S(1)} %copy-done.8), channel_id=1, source_target_pairs={{0,56},{8,64},{16,72},{24,80},{32,88},{40,96},{48,104},{56,112},{6... | collective-permute-start | bytes 3080 | tf_op jit(solution)/shard_map/ppermute | solution.py:16
  38.1 226.0 %collective-permute-start.10 = (s32[256]{0:T(256)S(1)}, s32[256]{0:T(256)S(1)}, u32[]{:S(2)}, u32[]{:S(2)}) collective-permute-start(s32[256]{0:T(256)S(1)} %copy-done.8), channel_id=1, source_target_pairs={{0,48},{8,56},{16,64},{24,72},{32,80},{40,88},{48,96},{56,104},{64... | collective-permute-start | bytes 3080 | tf_op jit(solution)/shard_map/ppermute | solution.py:16
  41.6 225.7 %collective-permute-start.11 = (s32[256]{0:T(256)S(1)}, s32[256]{0:T(256)S(1)}, u32[]{:S(2)}, u32[]{:S(2)}) collective-permute-start(s32[256]{0:T(256)S(1)} %copy-done.8), channel_id=1, source_target_pairs={{0,40},{8,48},{16,56},{24,64},{32,72},{40,80},{48,88},{56,96},{64,... | collective-permute-start | bytes 3080 | tf_op jit(solution)/shard_map/ppermute | solution.py:16
  46.8 220.5 %collective-permute-start.12 = (s32[256]{0:T(256)S(1)}, s32[256]{0:T(256)S(1)}, u32[]{:S(2)}, u32[]{:S(2)}) collective-permute-start(s32[256]{0:T(256)S(1)} %copy-done.8), channel_id=1, source_target_pairs={{0,32},{8,40},{16,48},{24,56},{32,64},{40,72},{48,80},{56,88},{64,... | collective-permute-start | bytes 3080 | tf_op jit(solution)/shard_map/ppermute | solution.py:16
  51.1 338.0 %reduce-scatter.3.cloned.1.call-start = ((), (), s32[]{:S(2)}) async-start(), calls=%async_computation.4 | async-start | bytes 1179648 | tf_op jit(solution)/shard_map/reduce_scatter | solution.py:110
  254.4 12.9 %collective-permute-start.13 = (s32[256]{0:T(256)S(1)}, s32[256]{0:T(256)S(1)}, u32[]{:S(2)}, u32[]{:S(2)}) collective-permute-start(s32[256]{0:T(256)S(1)} %copy-done.8), channel_id=1, source_target_pairs={{0,24},{8,32},{16,40},{24,48},{32,56},{40,64},{48,72},{56,80},{64,... | collective-permute-start | bytes 3080 | tf_op jit(solution)/shard_map/ppermute | solution.py:16
  257.2 10.1 %collective-permute-start.14 = (s32[256]{0:T(256)S(1)}, s32[256]{0:T(256)S(1)}, u32[]{:S(2)}, u32[]{:S(2)}) collective-permute-start(s32[256]{0:T(256)S(1)} %copy-done.8), channel_id=1, source_target_pairs={{0,16},{8,24},{16,32},{24,40},{32,48},{40,56},{48,64},{56,72},{64,... | collective-permute-start | bytes 3080 | tf_op jit(solution)/shard_map/ppermute | solution.py:16
  264.1 5.7 %collective-permute-start.15 = (s32[256]{0:T(256)S(1)}, s32[256]{0:T(256)S(1)}, u32[]{:S(2)}, u32[]{:S(2)}) collective-permute-start(s32[256]{0:T(256)S(1)} %copy-done.8), channel_id=1, source_target_pairs={{0,8},{8,16},{16,24},{24,32},{32,40},{40,48},{48,56},{56,64},{64,7... | collective-permute-start | bytes 3080 | tf_op jit(solution)/shard_map/ppermute | solution.py:16
  271.8 3.2 copy-start
  276.9 23.3 %collective-permute-start = (bf16[256,2,128]{0,2,1:T(8,128)(2,1)S(1)}, bf16[256,2,128]{0,2,1:T(8,128)(2,1)S(1)}, u32[]{:S(2)}, u32[]{:S(2)}) collective-permute-start(bf16[256,2,128]{0,2,1:T(8,128)(2,1)S(1)} %bitcast.17), channel_id=1, source_target_pairs={{0,64},{8,72},{16,80},{24,88},{32,96},{40,104},{48,112},{56,120},{... | collective-permute-start | bytes 393224 | tf_op jit(solution)/shard_map/ppermute | solution.py:16
  281.3 22.5 %collective-permute-start.1 = (bf16[256,2,128]{0,2,1:T(8,128)(2,1)S(1)}, bf16[256,2,128]{0,2,1:T(8,128)(2,1)S(1)}, u32[]{:S(2)}, u32[]{:S(2)}) collective-permute-start(bf16[256,2,128]{0,2,1:T(8,128)(2,1)S(1)} %bitcast.18), channel_id=1, source_target_pairs={{0,56},{8,64},{16,72},{24,80},{32,88},{40,96},{48,104},{56,112},{6... | collective-permute-start | bytes 393224 | tf_op jit(solution)/shard_map/ppermute | solution.py:16
  282.7 24.0 %collective-permute-start.2 = (bf16[256,2,128]{0,2,1:T(8,128)(2,1)S(1)}, bf16[256,2,128]{0,2,1:T(8,128)(2,1)S(1)}, u32[]{:S(2)}, u32[]{:S(2)}) collective-permute-start(bf16[256,2,128]{0,2,1:T(8,128)(2,1)S(1)} %bitcast.19), channel_id=1, source_target_pairs={{0,48},{8,56},{16,64},{24,72},{32,80},{40,88},{48,96},{56,104},{64... | collective-permute-start | bytes 393224 | tf_op jit(solution)/shard_map/ppermute | solution.py:16
  285.9 23.9 %collective-permute-start.3 = (bf16[256,2,128]{0,2,1:T(8,128)(2,1)S(1)}, bf16[256,2,128]{0,2,1:T(8,128)(2,1)S(1)}, u32[]{:S(2)}, u32[]{:S(2)}) collective-permute-start(bf16[256,2,128]{0,2,1:T(8,128)(2,1)S(1)} %bitcast.20), channel_id=1, source_target_pairs={{0,40},{8,48},{16,56},{24,64},{32,72},{40,80},{48,88},{56,96},{64,... | collective-permute-start | bytes 393224 | tf_op jit(solution)/shard_map/ppermute | solution.py:16
  293.3 18.9 %collective-permute-start.4 = (bf16[256,2,128]{0,2,1:T(8,128)(2,1)S(1)}, bf16[256,2,128]{0,2,1:T(8,128)(2,1)S(1)}, u32[]{:S(2)}, u32[]{:S(2)}) collective-permute-start(bf16[256,2,128]{0,2,1:T(8,128)(2,1)S(1)} %bitcast.21), channel_id=1, source_target_pairs={{0,32},{8,40},{16,48},{24,56},{32,64},{40,72},{48,80},{56,88},{64,... | collective-permute-start | bytes 393224 | tf_op jit(solution)/shard_map/ppermute | solution.py:16
  300.2 16.3 %collective-permute-start.5 = (bf16[256,2,128]{0,2,1:T(8,128)(2,1)S(1)}, bf16[256,2,128]{0,2,1:T(8,128)(2,1)S(1)}, u32[]{:S(2)}, u32[]{:S(2)}) collective-permute-start(bf16[256,2,128]{0,2,1:T(8,128)(2,1)S(1)} %bitcast.22), channel_id=1, source_target_pairs={{0,24},{8,32},{16,40},{24,48},{32,56},{40,64},{48,72},{56,80},{64,... | collective-permute-start | bytes 393224 | tf_op jit(solution)/shard_map/ppermute | solution.py:16
  303.9 15.4 %collective-permute-start.6 = (bf16[256,2,128]{0,2,1:T(8,128)(2,1)S(1)}, bf16[256,2,128]{0,2,1:T(8,128)(2,1)S(1)}, u32[]{:S(2)}, u32[]{:S(2)}) collective-permute-start(bf16[256,2,128]{0,2,1:T(8,128)(2,1)S(1)} %bitcast.23), channel_id=1, source_target_pairs={{0,16},{8,24},{16,32},{24,40},{32,48},{40,56},{48,64},{56,72},{64,... | collective-permute-start | bytes 393224 | tf_op jit(solution)/shard_map/ppermute | solution.py:16
  306.7 14.6 %collective-permute-start.7 = (bf16[256,2,128]{0,2,1:T(8,128)(2,1)S(1)}, bf16[256,2,128]{0,2,1:T(8,128)(2,1)S(1)}, u32[]{:S(2)}, u32[]{:S(2)}) collective-permute-start(bf16[256,2,128]{0,2,1:T(8,128)(2,1)S(1)} %bitcast.24), channel_id=1, source_target_pairs={{0,8},{8,16},{16,24},{24,32},{32,40},{40,48},{48,56},{56,64},{64,7... | collective-permute-start | bytes 393224 | tf_op jit(solution)/shard_map/ppermute | solution.py:16
  309.8 15.9 %collective-permute-start.16 = (bf16[256,2,128]{2,0,1:T(8,128)(2,1)S(1)}, bf16[256,2,128]{2,0,1:T(8,128)(2,1)S(1)}, u32[]{:S(2)}, u32[]{:S(2)}) collective-permute-start(bf16[256,2,128]{2,0,1:T(8,128)(2,1)S(1)} %maximum_convert_fusion), channel_id=1, source_target_pairs={{0,64},{8,72},{16,80},{24,88},{32,96},{40,104},{48,112},{56,120},{... | collective-permute-start | bytes 393224 | tf_op jit(solution)/shard_map/ppermute | solution.py:16
  312.1 16.3 %collective-permute-start.17 = (bf16[256,2,128]{2,0,1:T(8,128)(2,1)S(1)}, bf16[256,2,128]{2,0,1:T(8,128)(2,1)S(1)}, u32[]{:S(2)}, u32[]{:S(2)}) collective-permute-start(bf16[256,2,128]{2,0,1:T(8,128)(2,1)S(1)} %maximum_convert_fusion), channel_id=1, source_target_pairs={{0,56},{8,64},{16,72},{24,80},{32,88},{40,96},{48,104},{56,112},{6... | collective-permute-start | bytes 393224 | tf_op jit(solution)/shard_map/ppermute | solution.py:16
  316.5 14.8 %collective-permute-start.18 = (bf16[256,2,128]{2,0,1:T(8,128)(2,1)S(1)}, bf16[256,2,128]{2,0,1:T(8,128)(2,1)S(1)}, u32[]{:S(2)}, u32[]{:S(2)}) collective-permute-start(bf16[256,2,128]{2,0,1:T(8,128)(2,1)S(1)} %maximum_convert_fusion), channel_id=1, source_target_pairs={{0,48},{8,56},{16,64},{24,72},{32,80},{40,88},{48,96},{56,104},{64... | collective-permute-start | bytes 393224 | tf_op jit(solution)/shard_map/ppermute | solution.py:16
  319.3 15.4 %collective-permute-start.19 = (bf16[256,2,128]{2,0,1:T(8,128)(2,1)S(1)}, bf16[256,2,128]{2,0,1:T(8,128)(2,1)S(1)}, u32[]{:S(2)}, u32[]{:S(2)}) collective-permute-start(bf16[256,2,128]{2,0,1:T(8,128)(2,1)S(1)} %maximum_convert_fusion), channel_id=1, source_target_pairs={{0,40},{8,48},{16,56},{24,64},{32,72},{40,80},{48,88},{56,96},{64,... | collective-permute-start | bytes 393224 | tf_op jit(solution)/shard_map/ppermute | solution.py:16
  321.3 13.5 %collective-permute-start.20 = (bf16[256,2,128]{2,0,1:T(8,128)(2,1)S(1)}, bf16[256,2,128]{2,0,1:T(8,128)(2,1)S(1)}, u32[]{:S(2)}, u32[]{:S(2)}) collective-permute-start(bf16[256,2,128]{2,0,1:T(8,128)(2,1)S(1)} %maximum_convert_fusion), channel_id=1, source_target_pairs={{0,32},{8,40},{16,48},{24,56},{32,64},{40,72},{48,80},{56,88},{64,... | collective-permute-start | bytes 393224 | tf_op jit(solution)/shard_map/ppermute | solution.py:16
  325.6 12.0 %copy-start.5 = (bf16[2304,2,128]{0,2,1:T(8,128)(2,1)}, bf16[2304,2,128]{0,2,1:T(8,128)(2,1)S(1)}, u32[]{:S(2)}) copy-start(bf16[2304,2,128]{0,2,1:T(8,128)(2,1)S(1)} %constant_dynamic-update-slice_fusion.7) | copy-start | bytes 3538948
  325.7 9.2 %collective-permute-start.21 = (bf16[256,2,128]{2,0,1:T(8,128)(2,1)S(1)}, bf16[256,2,128]{2,0,1:T(8,128)(2,1)S(1)}, u32[]{:S(2)}, u32[]{:S(2)}) collective-permute-start(bf16[256,2,128]{2,0,1:T(8,128)(2,1)S(1)} %maximum_convert_fusion), channel_id=1, source_target_pairs={{0,24},{8,32},{16,40},{24,48},{32,56},{40,64},{48,72},{56,80},{64,... | collective-permute-start | bytes 393224 | tf_op jit(solution)/shard_map/ppermute | solution.py:16
  328.5 7.7 %collective-permute-start.22 = (bf16[256,2,128]{2,0,1:T(8,128)(2,1)S(1)}, bf16[256,2,128]{2,0,1:T(8,128)(2,1)S(1)}, u32[]{:S(2)}, u32[]{:S(2)}) collective-permute-start(bf16[256,2,128]{2,0,1:T(8,128)(2,1)S(1)} %maximum_convert_fusion), channel_id=1, source_target_pairs={{0,16},{8,24},{16,32},{24,40},{32,48},{40,56},{48,64},{56,72},{64,... | collective-permute-start | bytes 393224 | tf_op jit(solution)/shard_map/ppermute | solution.py:16
  331.3 6.3 %collective-permute-start.23 = (bf16[256,2,128]{2,0,1:T(8,128)(2,1)S(1)}, bf16[256,2,128]{2,0,1:T(8,128)(2,1)S(1)}, u32[]{:S(2)}, u32[]{:S(2)}) collective-permute-start(bf16[256,2,128]{2,0,1:T(8,128)(2,1)S(1)} %maximum_convert_fusion), channel_id=1, source_target_pairs={{0,8},{8,16},{16,24},{24,32},{32,40},{40,48},{48,56},{56,64},{64,7... | collective-permute-start | bytes 393224 | tf_op jit(solution)/shard_map/ppermute | solution.py:16
  337.7 1.0 copy-start.7
  338.7 6.1 %copy-start.6 = (bf16[2304,2,128]{0,2,1:T(8,128)(2,1)S(1)}, bf16[2304,2,128]{0,2,1:T(8,128)(2,1)}, u32[]{:S(2)}) copy-start(bf16[2304,2,128]{0,2,1:T(8,128)(2,1)} %copy-done.5) | copy-start | bytes 3538948
  348.1 41.1 %copy-start.4 = (bf16[256,256]{1,0:T(8,128)(2,1)S(1)}, bf16[256,256]{1,0:T(8,128)(2,1)}, u32[]{:S(2)}) copy-start(bf16[256,256]{1,0:T(8,128)(2,1)} %param.10) | copy-start | bytes 393220
  350.9 82.2 %all-gather.5.cloned.1.call-start = ((), (), s32[]{:S(2)}) async-start(), calls=%async_computation.5 | async-start | bytes 1179648 | tf_op jit(solution)/shard_map/all_gather | solution.py:114
  390.7 93.2 %reduce-scatter.5.cloned.1.call-start = ((), (), s32[]{:S(2)}) async-start(), calls=%async_computation.6 | async-start | bytes 1179648 | tf_op jit(solution)/shard_map/reduce_scatter | solution.py:122
  433.1 3.2 copy-start.1
  438.7 4.7 copy-start.9
  443.3 40.6 %copy-start.2 = (bf16[256,256]{1,0:T(8,128)(2,1)S(1)}, bf16[256,256]{1,0:T(8,128)(2,1)}, u32[]{:S(2)}) copy-start(bf16[256,256]{1,0:T(8,128)(2,1)} %add_convert_fusion.1) | copy-start | bytes 393220
  444.9 40.6 %copy-start.3 = (bf16[2,16,16,256]{3,2,1,0:T(8,128)(2,1)}, bf16[2,16,16,256]{3,2,1,0:T(8,128)(2,1)S(1)}, u32[]{:S(2)}) copy-start(bf16[2,16,16,256]{3,2,1,0:T(8,128)(2,1)S(1)} %scatter_fusion) | copy-start | bytes 786436
Sparse Core Ops, SparseCore 0:
  51.2 38.1 all-gather.2
  351.0 38.0 reduce-scatter.2
  391.7 41.3 all-gather.4
  443.5 40.3 reduce-scatter.4
